TPU v7x, 256 devices: a whole 4x4x8 slice. The times are simulated.
256 devices in a mesh: ctx: 16 (over z_lo, y), dp: 16 (over x, z_hi, core).
Axes of the slice: x: 4, y: 4, z: 8 (z_hi: 2, z_lo: 4; z = z_hi * 4 + z_lo), core: 2. Of those that a mesh axis runs over, the one named last changes fastest.
Arguments:
- inputs: bfloat16 [16, 2048, 4096], P('dp', 'ctx'), may hold values from -6 to 6
- b_proj: bfloat16 [16, 2048, 512], P('dp', 'ctx'), may hold values from -0.75 to 0.75
- c_proj: bfloat16 [16, 2048, 512], P('dp', 'ctx'), may hold values from -0.75 to 0.75
- dt_raw: float32 [16, 64, 2048], P('dp', None, 'ctx'), may hold values from -3 to 9
- a_log: float32 [64], P('dp'), may hold values from -12 to -3
- dt_bias: float32 [64], P('dp'), may hold values from 0.2 to 0.8
- d_skip: float32 [64], P('dp'), may hold values from 0.5 to 1.5
- grad_out: bfloat16 [16, 2048, 4096], P('dp', 'ctx'), may hold values from -6 to 6
Outputs:
- grad_inputs: bfloat16 [16, 2048, 4096], P('dp', 'ctx')
- grad_b: bfloat16 [16, 2048, 512], P('dp', 'ctx')
- grad_c: bfloat16 [16, 2048, 512], P('dp', 'ctx')
- grad_dt: float32 [16, 64, 2048], P('dp', None, 'ctx')
- grad_alog: float32 [64], P('dp')
- grad_bias: float32 [64], P('dp')
- grad_skip: float32 [64], P('dp')
All inputs are finite; a program needn't handle non-finite values.
Results may differ from a plain program's by a relative error of at most 0.0014.
Values sent between devices are 32-bit elements; how exact they have to be, the bound alone decides.
No kernel may reach another device: no remote copies, remote signals or barrier semaphores. Data moves between devices by JAX's collectives and lax.ppermute only.
A program may use at most 192 MiB of HBM per device.

v0:
```python
import jax
import jax.numpy as jnp
from jax import lax
from jax.sharding import PartitionSpec as P

P_SIZE = 64
N = 64
G = 8
highest = lax.Precision.HIGHEST


def slab_scan(x, b, c, raw, bias, alog, skip, state_in):
    tokens, num_heads, width = x.shape
    group_heads = num_heads // G
    dt_value = jax.nn.softplus(raw + bias[:, None])
    log_decay = dt_value * (-jnp.exp(alog))[:, None]
    cumulative = jnp.cumsum(log_decay, axis=1)
    scaled = (x * dt_value.T[:, :, None]).reshape(tokens, G, group_heads, width)
    scores = jnp.einsum("qgn,kgn->gqk", c, b, precision=highest)
    offsets = jnp.arange(tokens)
    causal = offsets[:, None] >= offsets[None, :]
    spread = cumulative[:, :, None] - cumulative[:, None, :]
    weights = jnp.where(causal, jnp.exp(jnp.where(causal, spread, 0.0)), 0.0)
    mixed = weights.reshape(G, group_heads, tokens, tokens) * scores[:, None]
    local_part = jnp.einsum("gjqk,kgjp->qgjp", mixed, scaled, precision=highest)
    tail_decay = jnp.exp(cumulative[:, -1:] - cumulative)
    weighted_b = b[:, :, None, :] * tail_decay.T.reshape(tokens, G, group_heads)[:, :, :, None]
    block_state = jnp.einsum("kgjn,kgjp->gjpn", weighted_b, scaled, precision=highest)
    block_state = block_state.reshape(num_heads, width, N)
    state_out = jnp.exp(cumulative[:, -1])[:, None, None] * state_in + block_state
    entering = state_in.reshape(G, group_heads, width, N)
    cross_part = jnp.einsum("qgn,gjpn->qgjp", c, entering, precision=highest)
    cross_part = cross_part * jnp.exp(cumulative).T.reshape(tokens, G, group_heads)[:, :, :, None]
    result = (local_part + cross_part).reshape(tokens, num_heads, width)
    result = result + skip[None, :, None] * x
    return (result, state_out)


def slab_terms(x, b, c, raw, bias, alog, grad):
    tokens, num_heads, width = x.shape
    group_heads = num_heads // G
    dt_value = jax.nn.softplus(raw + bias[:, None])
    log_decay = dt_value * (-jnp.exp(alog))[:, None]
    cumulative = jnp.cumsum(log_decay, axis=1)
    total = cumulative[:, -1]
    tail_decay = jnp.exp(total[:, None] - cumulative)
    carried = (x * (dt_value * tail_decay).T[:, :, None]).reshape(tokens, G, group_heads, width)
    local_state = jnp.einsum("tgn,tgjp->gjpn", b, carried, precision=highest)
    weighted_grad = (grad * jnp.exp(cumulative).T[:, :, None]).reshape(
        tokens, G, group_heads, width
    )
    local_source = jnp.einsum("tgn,tgjp->gjpn", c, weighted_grad, precision=highest)
    return (
        total,
        local_state.reshape(num_heads, width, N),
        local_source.reshape(num_heads, width, N),
    )


def carry_across(total, local_state, local_source):
    count = lax.axis_size("ctx")
    num_heads = total.shape[0]
    share = num_heads // count
    lanes = local_state.shape[2]
    payload = jnp.concatenate(
        [local_state, local_source, jnp.broadcast_to(total[:, None, None], (num_heads, 1, lanes))],
        axis=1,
    )
    got = lax.all_to_all(payload, "ctx", 0, 0, tiled=True)
    got = got.reshape(count, share, got.shape[1], lanes)
    width = local_state.shape[1]
    states = got[:, :, :width].reshape(count, share, width * lanes)
    sources = got[:, :, width : 2 * width].reshape(count, share, width * lanes)
    totals = got[:, :, 2 * width, 0]
    slab = jnp.arange(count)
    between = (slab[None, :, None] < slab[None, None, :]) & (
        slab[None, None, :] < slab[:, None, None]
    )
    exponent = jnp.einsum("jim,mh->jih", between.astype(jnp.float32), totals, precision=highest)
    before = slab[None, :] < slab[:, None]
    chain = jnp.where(
        before[:, :, None], jnp.exp(jnp.where(before[:, :, None], exponent, 0.0)), 0.0
    )
    entering = jnp.einsum("jih,ihx->jhx", chain, states, precision=highest)
    leaving = jnp.einsum("jkh,jhx->khx", chain, sources, precision=highest)
    back = jnp.concatenate(
        [
            entering.reshape(count * share, width, lanes),
            leaving.reshape(count * share, width, lanes),
        ],
        axis=1,
    )
    mine = lax.all_to_all(back, "ctx", 0, 0, tiled=True)
    return (mine[:, :width], mine[:, width:])


def per_device(inputs, b_proj, c_proj, dt_raw, a_log, dt_bias, d_skip, grad_out):
    params = lax.all_gather(jnp.stack([a_log, dt_bias, d_skip]), "dp", axis=1, tiled=True)
    alog_all, bias_all, skip_all = (params[0], params[1], params[2])
    tokens = inputs.shape[1]
    num_heads = alog_all.shape[0]
    x = inputs[0].astype(jnp.float32).reshape(tokens, num_heads, P_SIZE)
    grad = grad_out[0].astype(jnp.float32).reshape(tokens, num_heads, P_SIZE)
    b = b_proj[0].astype(jnp.float32).reshape(tokens, G, N)
    c = c_proj[0].astype(jnp.float32).reshape(tokens, G, N)
    raw = dt_raw[0]
    total, local_state, local_source = slab_terms(x, b, c, raw, bias_all, alog_all, grad)
    entering, leaving = carry_across(total, local_state, local_source)
    _, pullback = jax.vjp(slab_scan, x, b, c, raw, bias_all, alog_all, skip_all, entering)
    gx, gb, gc, graw, gbias, galog, gskip, _ = pullback((grad, leaving))
    grad_inputs = gx.reshape(tokens, num_heads * P_SIZE).astype(jnp.bfloat16)[None]
    grad_b = gb.reshape(tokens, G * N).astype(jnp.bfloat16)[None]
    grad_c = gc.reshape(tokens, G * N).astype(jnp.bfloat16)[None]
    grad_dt = graw[None]
    head_stats = jnp.stack([galog, gbias, gskip], axis=0)
    share_size = num_heads // lax.axis_size("dp")
    summed = lax.psum(head_stats, ("ctx", "dp"))
    own_totals = lax.dynamic_slice_in_dim(summed, lax.axis_index("dp") * share_size, share_size, 1)
    return (grad_inputs, grad_b, grad_c, grad_dt, own_totals[0], own_totals[1], own_totals[2])


def solution(mesh):
    in_specs = (
        P("dp", "ctx", None),
        P("dp", "ctx", None),
        P("dp", "ctx", None),
        P("dp", None, "ctx"),
        P("dp"),
        P("dp"),
        P("dp"),
        P("dp", "ctx", None),
    )
    out_specs = (
        P("dp", "ctx", None),
        P("dp", "ctx", None),
        P("dp", "ctx", None),
        P("dp", None, "ctx"),
        P("dp"),
        P("dp"),
        P("dp"),
    )
    return jax.shard_map(
        per_device, mesh=mesh, in_specs=in_specs, out_specs=out_specs, check_vma=False
    )
```

profile of v0, /device:TPU:1, one launch (start us, length us, event | category | flops | bytes accessed | tf_op | source)
XLA Modules:
  0.0 347.0 jit_solution(9068073911150541548)
XLA Ops:
  1.5 34.5 %all-gather = f32[16,4,3]{2,1,0:T(4,128)S(1)} all-gather(f32[1,4,3]{2,1,0:T(4,128)S(1)} %bitcast.241), channel_id=1, replica_groups=mesh['ctx'=16,'dp'=16] {'dp'}, dimensions={0}, use_global_device_ids=true | all-gather | bytes 816 | tf_op jit(solution)/shard_map/all_gather | solution.py:98
  43.2 3.9 %fusion.9 = f32[8,8,64,64]{2,3,1,0:T(8,128)S(1)} fusion(bf16[128,8,64,1]{0,2,3,1:T(8,128)(2,1)S(1)} %bitcast.214, bf16[128,8,8,64]{0,3,2,1:T(8,128)(2,1)S(1)} %bitcast.198, f32[128,8,8]{0,2,1:T(8,128)} %bitcast.224), kind=kOutput, calls=%fused_computation.19 | convolution fusion | flops 403701760 | bytes 2260992 | tf_op jit(solution)/shard_map/tgn,tgjp->gjpn/dot_general | solution.py:52
  47.1 3.1 fusion.26
  50.5 3.2 pad_maximum_fusion
  53.6 5.7 %all-to-all-start = ((f32[64,129,64]{1,2,0:T(8,128)}), f32[64,129,64]{1,2,0:T(8,128)}, u32[]{:S(2)}, u32[]{:S(2)}) async-start(f32[64,129,64]{1,2,0:T(8,128)} %pad_maximum_fusion), calls=%async_computation | async-start | bytes 8388608 | tf_op jit(solution)/shard_map/all_to_all | solution.py:69
  59.4 78.3 %all-to-all-done = f32[64,129,64]{1,2,0:T(8,128)} async-done(((f32[64,129,64]{1,2,0:T(8,128)}), f32[64,129,64]{1,2,0:T(8,128)}, u32[]{:S(2)}, u32[]{:S(2)}) %all-to-all-start) | async-done | bytes 2113568 | tf_op jit(solution)/shard_map/all_to_all | solution.py:69
  138.7 4.9 %fusion.68 = (f32[16,4,64,64]{2,3,1,0:T(8,128)}, f32[16,4,64,64]{2,3,1,0:T(8,128)}) fusion(f32[16,4,129,64]{2,3,1,0:T(8,128)} %bitcast.26), kind=kLoop, calls=%fused_computation.110 | loop fusion | bytes 4194304 | tf_op jit(solution)/shard_map/slice | solution.py:72
  145.0 3.0 copy.200
  148.0 2.1 reshape.270
  152.6 2.4 reshape.271
  154.9 3.0 copy.204
  162.5 2.3 reshape.273
  164.8 4.7 %pad_maximum_fusion.1 = f32[64,128,64]{2,1,0:T(8,128)} fusion(f32[64,64,64]{2,1,0:T(8,128)} %reshape.273, f32[64,64,64]{2,1,0:T(8,128)} %reshape.271), kind=kLoop, calls=%fused_computation.3 | loop fusion | flops 524288 | bytes 4194304 | tf_op jit(solution)/shard_map/concatenate | solution.py:86
  169.5 3.8 %copy.207 = f32[64,128,64]{1,2,0:T(8,128)} copy(f32[64,128,64]{2,1,0:T(8,128)} %pad_maximum_fusion.1) | data formatting | bytes 4194304 | tf_op jit(solution)/shard_map/concatenate | solution.py:86
  173.4 19.6 %all-to-all-start.1 = ((f32[64,128,64]{1,2,0:T(8,128)}), f32[64,128,64]{1,2,0:T(8,128)}, u32[]{:S(2)}, u32[]{:S(2)}) async-start(f32[64,128,64]{1,2,0:T(8,128)} %copy.207), calls=%async_computation.1 | async-start | bytes 4194304 | tf_op jit(solution)/shard_map/all_to_all | solution.py:93
  193.5 7.1 %fusion.11 = (f32[8,8,128]{2,1,0:T(8,128)S(1)}, f32[8,8,128]{2,1,0:T(8,128)}, f32[8,128,128]{1,2,0:T(8,128)}) fusion(f32[8,128,128]{1,2,0:T(8,128)S(1)} %fusion.72, f32[8,8,128]{2,1,0:T(8,128)S(1)} %bitcast.235, pred[128,128]{0,1:T(8,128)(4,1)S(1)} %iota_compare_fusion, bf16[8,8,64,128]{3,2,1,0:T(8,128)(2,1)S(1)} %bitcast.199, ...), kind=kOutput, calls=%fused_computation.21 | convolution fusion | flops 817741824 | bytes 3293184 | tf_op jit(solution)/shard_map/transpose(jvp(gjqk,kgjp->qgjp))/dot_general | solution.py:25
  201.6 6.2 %fusion.4 = f32[8,8,128,64]{2,3,1,0:T(8,128)} fusion(bf16[8,8,64,128]{3,2,1,0:T(8,128)(2,1)S(1)} %bitcast.200, f32[8,128,128]{1,2,0:T(8,128)S(1)} %fusion.72, f32[8,8,128]{2,1,0:T(8,128)S(1)} %bitcast.236, pred[128,128]{0,1:T(8,128)(4,1)S(1)} %iota_compare_fusion), kind=kOutput, calls=%fused_computation.10 | convolution fusion | flops 809500672 | bytes 3719168 | tf_op jit(solution)/shard_map/transpose(jvp(gjqk,kgjp->qgjp))/dot_general | solution.py:25
  207.8 26.7 %all-to-all-done.1 = f32[64,128,64]{1,2,0:T(8,128)} async-done(((f32[64,128,64]{1,2,0:T(8,128)}), f32[64,128,64]{1,2,0:T(8,128)}, u32[]{:S(2)}, u32[]{:S(2)}) %all-to-all-start.1) | async-done | bytes 2097184 | tf_op jit(solution)/shard_map/all_to_all | solution.py:93
  234.6 3.7 %multiply_reduce_fusion = (f32[64]{0:T(128)S(1)}, f32[64,64,64]{1,2,0:T(8,128)S(1)}, f32[64,64,64]{1,2,0:T(8,128)S(1)}) fusion(f32[64,128,64]{1,2,0:T(8,128)} %all-to-all-done.1), kind=kLoop, calls=%fused_computation.33 | loop fusion | flops 524224 | bytes 4194560 | tf_op jit(solution)/shard_map/transpose(jvp())/reduce_sum | solution.py:30
  240.1 2.9 fusion.36
  243.0 3.2 fusion.19
  248.1 7.3 %multiply_reduce_fusion.1 = (f32[128,8,8]{0,2,1:T(8,128)S(1)}, f32[128,8,8,64]{0,3,2,1:T(8,128)}) fusion(f32[8,8,128,64]{2,3,1,0:T(8,128)} %fusion.4, f32[8,8,64,64]{2,3,1,0:T(8,128)} %bitcast.208, f32[128,8,8]{0,2,1:T(8,128)S(1)} %bitcast.227, f32[128,8,64]{0,2,1:T(8,128)S(1)} %convert_element_type.70, bf16[128,8,8,64]{0,3,2,1:T(8,128)(2,1)S(1)} %bitcast.206), kind=kOutput, calls=%fused_computation.34 | convolution fusion | flops 405266432 | bytes 6619136 | tf_op jit(solution)/shard_map/transpose(jvp(kgjn,kgjp->gjpn))/dot_general | solution.py:28
  256.3 2.5 fusion.16
  259.1 80.5 %psum.7 = f32[3,64]{1,0:T(4,128)S(1)} all-reduce(f32[3,64]{1,0:T(4,128)S(1)} %pad_maximum_fusion.2), channel_id=1, replica_groups=mesh['ctx'=16,'dp'=16] {'ctx','dp'}, use_global_device_ids=true, to_apply=%region_15.16 | all-reduce | flops 192 | bytes 1536 | tf_op jit(solution)/shard_map/psum | solution.py:117
  (101 shorter events, 31.0 us)
Async XLA Ops:
  0.6 40.0 %copy-start.11 = (bf16[1,128,512]{2,1,0:T(8,128)(2,1)S(1)}, bf16[1,128,512]{2,1,0:T(8,128)(2,1)}, u32[]{:S(2)}) copy-start(bf16[1,128,512]{2,1,0:T(8,128)(2,1)} %param.10) | copy-start | bytes 393220
  0.6 40.8 %copy-start.1 = (bf16[1,128,4096]{2,1,0:T(8,128)(2,1)S(1)}, bf16[1,128,4096]{2,1,0:T(8,128)(2,1)}, u32[]{:S(2)}) copy-start(bf16[1,128,4096]{2,1,0:T(8,128)(2,1)} %param.8) | copy-start | bytes 3145732
  36.2 0.9 copy-start.16
  36.2 0.9 copy-start.18
  36.2 2.8 copy-start.14
  37.5 1.5 copy-start.9
  37.6 12.6 %copy-start.12 = (f32[64]{0:T(128)}, f32[64]{0:T(128)S(1)}, u32[]{:S(2)}) copy-start(f32[64]{0:T(128)S(1)} %slice_bitcast_fusion.5) | copy-start | bytes 772
  42.2 4.9 %copy-start.8 = (f32[128,64]{0,1:T(8,128)S(1)}, f32[128,64]{0,1:T(8,128)}, u32[]{:S(2)}) copy-start(f32[128,64]{0,1:T(8,128)} %copy.194) | copy-start | bytes 98308
  53.6 84.1 %all-to-all-start = ((f32[64,129,64]{1,2,0:T(8,128)}), f32[64,129,64]{1,2,0:T(8,128)}, u32[]{:S(2)}, u32[]{:S(2)}) async-start(f32[64,129,64]{1,2,0:T(8,128)} %pad_maximum_fusion), calls=%async_computation | async-start | bytes 8388608 | tf_op jit(solution)/shard_map/all_to_all | solution.py:69
  173.4 19.6 %copy-start.6 = (f32[128,64]{1,0:T(8,128)S(1)}, f32[128,64]{1,0:T(8,128)}, u32[]{:S(2)}) copy-start(f32[128,64]{1,0:T(8,128)} %get-tuple-element.71) | copy-start | bytes 98308
  173.4 19.7 %copy-start.5 = (f32[128,64]{1,0:T(8,128)S(1)}, f32[128,64]{1,0:T(8,128)}, u32[]{:S(2)}) copy-start(f32[128,64]{1,0:T(8,128)} %get-tuple-element.73) | copy-start | bytes 98308
  173.4 20.1 %copy-start.10 = (f32[64,128]{1,0:T(8,128)S(1)}, f32[64,128]{1,0:T(8,128)}, u32[]{:S(2)}) copy-start(f32[64,128]{1,0:T(8,128)} %copy-done.9) | copy-start | bytes 98308
  173.4 61.2 %all-to-all-start.1 = ((f32[64,128,64]{1,2,0:T(8,128)}), f32[64,128,64]{1,2,0:T(8,128)}, u32[]{:S(2)}, u32[]{:S(2)}) async-start(f32[64,128,64]{1,2,0:T(8,128)} %copy.207), calls=%async_computation.1 | async-start | bytes 4194304 | tf_op jit(solution)/shard_map/all_to_all | solution.py:93
  193.1 50.0 %copy-start.3 = (f32[128,64]{0,1:T(8,128)}, f32[128,64]{0,1:T(8,128)S(1)}, u32[]{:S(2)}) copy-start(f32[128,64]{0,1:T(8,128)S(1)} %copy.212) | copy-start | bytes 98308
  238.3 4.8 %copy-start = (f32[64,64,64]{1,2,0:T(8,128)}, f32[64,64,64]{1,2,0:T(8,128)S(1)}, u32[]{:S(2)}) copy-start(f32[64,64,64]{1,2,0:T(8,128)S(1)} %get-tuple-element.67) | copy-start | bytes 3145732
  238.3 1.8 copy-start.2
  243.0 3.3 copy-start.13
  248.0 7.4 %copy-start.15 = (f32[64]{0:T(128)S(1)}, f32[64]{0:T(128)}, u32[]{:S(2)}) copy-start(f32[64]{0:T(128)} %copy-done.14) | copy-start | bytes 772
  248.0 7.4 %copy-start.19 = (f32[64]{0:T(128)S(1)}, f32[64]{0:T(128)}, u32[]{:S(2)}) copy-start(f32[64]{0:T(128)} %copy-done.18) | copy-start | bytes 772
  248.0 8.1 %copy-start.17 = (f32[64,3]{0,1:T(4,128)S(1)}, f32[64,3]{0,1:T(4,128)}, u32[]{:S(2)}) copy-start(f32[64,3]{0,1:T(4,128)} %copy-done.16) | copy-start | bytes 2308
  248.0 8.3 %copy-start.4 = (f32[128,64]{0,1:T(8,128)S(1)}, f32[128,64]{0,1:T(8,128)}, u32[]{:S(2)}) copy-start(f32[128,64]{0,1:T(8,128)} %copy-done.3) | copy-start | bytes 98308
  341.7 4.6 %copy-start.7 = (f32[64,128]{0,1:T(8,128)S(1)}, f32[64,128]{0,1:T(8,128)}, u32[]{:S(2)}) copy-start(f32[64,128]{0,1:T(8,128)} %get-tuple-element.62) | copy-start | bytes 98308
where the time goes:
time: 348 us; the launch traced here: 347 us
  blocking collectives  115 us (33%)
  waiting for transfers between devices  105 us (30%)
  matrix products  43.3 us (12%)
  local copies, waits for them, and re-layouts  38.9 us (11%)
  starting transfers between devices  25.3 us (7%)
  other arithmetic  18.2 us (5%)
    psum x1, blocking collectives, per_device(): summed = lax.psum(head_stats, ('ctx', 'dp'))  80.5 us
    all_to_all x1, waiting for transfers between devices, carry_across(): got = lax.all_to_all(payload, 'ctx', 0, 0, tiled=True)  78.3 us
    all_gather x1, blocking collectives, per_device(): lax.all_gather(jnp.stack([a_log, dt_bias, d_skip]), 'dp', axis=1, tiled=T...  34.5 us
    all_to_all x1, waiting for transfers between devices, carry_across(): mine = lax.all_to_all(back, 'ctx', 0, 0, tiled=True)  26.7 us
    all_to_all x1, starting transfers between devices, carry_across(): mine = lax.all_to_all(back, 'ctx', 0, 0, tiled=True)  19.6 us
    dot_general x2, matrix products, slab_scan(): local_part = jnp.einsum('gjqk,kgjp->qgjp', mixed, scaled, precision=highest)  13.3 us
    dot_general x2, matrix products, slab_scan(): jnp.einsum('kgjn,kgjp->gjpn', weighted_b, scaled, precision=highest)  10.5 us
    unnamed x51, local copies, waits for them, and re-layouts  8.07 us
  transfers between devices with their start and end apart: 2, of which 2 were waited for; matrix products, arithmetic and copies ran while one was open for 4% of the time, Pallas kernels for 0%

commit v1 on v0

--- a/solution.py
+++ b/solution.py
@@ -95,7 +95,12 @@
 
 
 def per_device(inputs, b_proj, c_proj, dt_raw, a_log, dt_bias, d_skip, grad_out):
-    params = lax.all_gather(jnp.stack([a_log, dt_bias, d_skip]), "dp", axis=1, tiled=True)
+    params = jnp.concatenate(
+        lax.all_to_all(
+            jnp.stack([jnp.stack([a_log, dt_bias, d_skip])] * lax.axis_size("dp")), "dp", 0, 0
+        ),
+        axis=1,
+    )
     alog_all, bias_all, skip_all = (params[0], params[1], params[2])
     tokens = inputs.shape[1]
     num_heads = alog_all.shape[0]

time: 348 us -> 332 us (0.954)
  blocking collectives: 115 us -> 80.5 us
  starting transfers between devices: 25.3 us -> 37.8 us
  waiting for transfers between devices: 105 us -> 109 us
    all_gather x1 -> x0, blocking collectives: 34.5 us -> none  [per_device(): lax.all_gather(jnp.stack([a_log, dt_bias, d_skip]), 'dp', axis=1, tiled=T...]
    all_to_all x0 -> x1, starting transfers between devices: none -> 12.4 us  [per_device(): lax.all_to_all(jnp.stack([jnp.stack([a_log, dt_bias, d_skip])] * lax.axis...]
    all_to_all x0 -> x1, waiting for transfers between devices: none -> 5.39 us  [per_device(): lax.all_to_all(jnp.stack([jnp.stack([a_log, dt_bias, d_skip])] * lax.axis...]
    unnamed x51 -> x49, local copies, waits for them, and re-layouts: 8.07 us -> 8.3 us
  transfers between devices with their start and end apart: 2 -> 3, of which waited for: 2 -> 3; matrix products, arithmetic and copies ran while one was open for 4% -> 6% of each run, Pallas kernels for 0% -> 0%
where the time goes in v1:
time: 332 us; the launch traced here: 331 us
  waiting for transfers between devices  109 us (33%)
  blocking collectives  80.5 us (24%)
  matrix products  43.1 us (13%)
  local copies, waits for them, and re-layouts  40.6 us (12%)
  starting transfers between devices  37.8 us (11%)
  other arithmetic  18.6 us (6%)
    psum x1, blocking collectives, per_device(): summed = lax.psum(head_stats, ('ctx', 'dp'))  80.5 us
    all_to_all x1, waiting for transfers between devices, carry_across(): got = lax.all_to_all(payload, 'ctx', 0, 0, tiled=True)  78.3 us
    all_to_all x1, waiting for transfers between devices, carry_across(): mine = lax.all_to_all(back, 'ctx', 0, 0, tiled=True)  25.2 us
    all_to_all x1, starting transfers between devices, carry_across(): mine = lax.all_to_all(back, 'ctx', 0, 0, tiled=True)  19.6 us
    dot_general x2, matrix products, slab_scan(): local_part = jnp.einsum('gjqk,kgjp->qgjp', mixed, scaled, precision=highest)  14.1 us
    all_to_all x1, starting transfers between devices, per_device(): lax.all_to_all(jnp.stack([jnp.stack([a_log, dt_bias, d_skip])] * lax.axis...  12.4 us
    dot_general x2, matrix products, slab_scan(): jnp.einsum('kgjn,kgjp->gjpn', weighted_b, scaled, precision=highest)  10.5 us
    unnamed x49, local copies, waits for them, and re-layouts  8.3 us
  transfers between devices with their start and end apart: 3, of which 3 were waited for; matrix products, arithmetic and copies ran while one was open for 6% of the time, Pallas kernels for 0%

profile of v1, /device:TPU:1, one launch (start us, length us, event | category | flops | bytes accessed | tf_op | source)
XLA Modules:
  0.0 330.5 jit_solution(4749987517133839716)
XLA Ops:
  2.1 12.4 %all-to-all-start = ((f32[16,3,4]{2,1,0:T(4,128)}), f32[16,3,4]{2,1,0:T(4,128)S(1)}, u32[]{:S(2)}, u32[]{:S(2)}) async-start(f32[16,3,4]{2,1,0:T(4,128)} %stack.20), calls=%async_computation | async-start | bytes 65536 | tf_op jit(solution)/shard_map/all_to_all | solution.py:99
  18.8 5.4 %all-to-all-done = f32[16,3,4]{2,1,0:T(4,128)S(1)} async-done(((f32[16,3,4]{2,1,0:T(4,128)}), f32[16,3,4]{2,1,0:T(4,128)S(1)}, u32[]{:S(2)}, u32[]{:S(2)}) %all-to-all-start) | async-done | bytes 800 | tf_op jit(solution)/shard_map/all_to_all | solution.py:99
  26.3 3.2 fusion.9
  29.5 3.1 fusion.26
  32.8 3.2 pad_maximum_fusion
  36.0 5.7 %all-to-all-start.1 = ((f32[64,129,64]{1,2,0:T(8,128)}), f32[64,129,64]{1,2,0:T(8,128)}, u32[]{:S(2)}, u32[]{:S(2)}) async-start(f32[64,129,64]{1,2,0:T(8,128)} %pad_maximum_fusion), calls=%async_computation.1 | async-start | bytes 8388608 | tf_op jit(solution)/shard_map/all_to_all | solution.py:69
  41.8 78.3 %all-to-all-done.1 = f32[64,129,64]{1,2,0:T(8,128)} async-done(((f32[64,129,64]{1,2,0:T(8,128)}), f32[64,129,64]{1,2,0:T(8,128)}, u32[]{:S(2)}, u32[]{:S(2)}) %all-to-all-start.1) | async-done | bytes 2113568 | tf_op jit(solution)/shard_map/all_to_all | solution.py:69
  121.0 4.9 %fusion.69 = (f32[16,4,64,64]{2,3,1,0:T(8,128)}, f32[16,4,64,64]{2,3,1,0:T(8,128)}) fusion(f32[16,4,129,64]{2,3,1,0:T(8,128)} %bitcast.20), kind=kLoop, calls=%fused_computation.111 | loop fusion | bytes 4194304 | tf_op jit(solution)/shard_map/slice | solution.py:72
  127.3 3.0 copy.161
  134.9 2.4 reshape.298
  137.2 3.0 copy.165
  144.8 2.3 reshape.300
  147.1 4.7 %pad_maximum_fusion.1 = f32[64,128,64]{2,1,0:T(8,128)} fusion(f32[64,64,64]{2,1,0:T(8,128)} %reshape.300, f32[64,64,64]{2,1,0:T(8,128)} %reshape.298), kind=kLoop, calls=%fused_computation.3 | loop fusion | flops 524288 | bytes 4194304 | tf_op jit(solution)/shard_map/concatenate | solution.py:86
  151.8 3.8 %copy.168 = f32[64,128,64]{1,2,0:T(8,128)} copy(f32[64,128,64]{2,1,0:T(8,128)} %pad_maximum_fusion.1) | data formatting | bytes 4194304 | tf_op jit(solution)/shard_map/concatenate | solution.py:86
  155.6 19.6 %all-to-all-start.2 = ((f32[64,128,64]{1,2,0:T(8,128)}), f32[64,128,64]{1,2,0:T(8,128)}, u32[]{:S(2)}, u32[]{:S(2)}) async-start(f32[64,128,64]{1,2,0:T(8,128)} %copy.168), calls=%async_computation.2 | async-start | bytes 4194304 | tf_op jit(solution)/shard_map/all_to_all | solution.py:93
  175.8 7.1 %fusion.11 = (f32[8,8,128]{2,1,0:T(8,128)S(1)}, f32[8,8,128]{2,1,0:T(8,128)}, f32[8,128,128]{1,2,0:T(8,128)}) fusion(f32[8,128,128]{1,2,0:T(8,128)S(1)} %fusion.73, f32[8,8,128]{2,1,0:T(8,128)S(1)} %bitcast.225, pred[128,128]{0,1:T(8,128)(4,1)S(1)} %iota_compare_fusion, bf16[8,8,64,128]{3,2,1,0:T(8,128)(2,1)S(1)} %bitcast.189, ...), kind=kOutput, calls=%fused_computation.21 | convolution fusion | flops 817741824 | bytes 3293184 | tf_op jit(solution)/shard_map/transpose(jvp(gjqk,kgjp->qgjp))/dot_general | solution.py:25
  184.8 6.9 %fusion.4 = f32[8,8,128,64]{2,3,1,0:T(8,128)} fusion(bf16[8,8,64,128]{3,2,1,0:T(8,128)(2,1)S(1)} %bitcast.190, f32[8,128,128]{1,2,0:T(8,128)S(1)} %fusion.73, f32[8,8,128]{2,1,0:T(8,128)S(1)} %bitcast.226, pred[128,128]{0,1:T(8,128)(4,1)} %copy-done.12), kind=kOutput, calls=%fused_computation.10 | convolution fusion | flops 809500672 | bytes 3719168 | tf_op jit(solution)/shard_map/transpose(jvp(gjqk,kgjp->qgjp))/dot_general | solution.py:25
  191.7 25.2 %all-to-all-done.2 = f32[64,128,64]{1,2,0:T(8,128)} async-done(((f32[64,128,64]{1,2,0:T(8,128)}), f32[64,128,64]{1,2,0:T(8,128)}, u32[]{:S(2)}, u32[]{:S(2)}) %all-to-all-start.2) | async-done | bytes 2097184 | tf_op jit(solution)/shard_map/all_to_all | solution.py:93
  216.8 3.7 %multiply_reduce_fusion = (f32[64]{0:T(128)S(1)}, f32[64,64,64]{1,2,0:T(8,128)S(1)}, f32[64,64,64]{1,2,0:T(8,128)S(1)}) fusion(f32[64,128,64]{1,2,0:T(8,128)} %all-to-all-done.2), kind=kLoop, calls=%fused_computation.33 | loop fusion | flops 524224 | bytes 4194560 | tf_op jit(solution)/shard_map/transpose(jvp())/reduce_sum | solution.py:30
  222.4 2.9 fusion.36
  225.3 3.2 fusion.19
  230.9 7.3 %multiply_reduce_fusion.1 = (f32[128,8,8]{0,2,1:T(8,128)S(1)}, f32[128,8,8,64]{0,3,2,1:T(8,128)}) fusion(f32[8,8,128,64]{2,3,1,0:T(8,128)} %fusion.4, f32[8,8,64,64]{2,3,1,0:T(8,128)} %bitcast.198, f32[128,8,8]{0,2,1:T(8,128)S(1)} %bitcast.217, f32[128,8,64]{0,2,1:T(8,128)S(1)} %convert_element_type.70, bf16[128,8,8,64]{0,3,2,1:T(8,128)(2,1)S(1)} %bitcast.196), kind=kOutput, calls=%fused_computation.34 | convolution fusion | flops 405266432 | bytes 6619136 | tf_op jit(solution)/shard_map/transpose(jvp(kgjn,kgjp->gjpn))/dot_general | solution.py:28
  239.0 2.6 fusion.16
  242.8 80.5 %psum.7 = f32[3,64]{1,0:T(4,128)S(1)} all-reduce(f32[3,64]{1,0:T(4,128)S(1)} %pad_maximum_fusion.3), channel_id=1, replica_groups=mesh['ctx'=16,'dp'=16] {'ctx','dp'}, use_global_device_ids=true, to_apply=%region_15.16 | all-reduce | flops 192 | bytes 1536 | tf_op jit(solution)/shard_map/psum | solution.py:122
  (105 shorter events, 35.0 us)
Async XLA Ops:
  0.6 16.3 %copy-start.11 = (bf16[1,128,512]{2,1,0:T(8,128)(2,1)S(1)}, bf16[1,128,512]{2,1,0:T(8,128)(2,1)}, u32[]{:S(2)}) copy-start(bf16[1,128,512]{2,1,0:T(8,128)(2,1)} %param.10) | copy-start | bytes 393220
  0.6 16.5 %copy-start.2 = (bf16[1,128,4096]{2,1,0:T(8,128)(2,1)S(1)}, bf16[1,128,4096]{2,1,0:T(8,128)(2,1)}, u32[]{:S(2)}) copy-start(bf16[1,128,4096]{2,1,0:T(8,128)(2,1)} %param.8) | copy-start | bytes 3145732
  2.1 22.1 %all-to-all-start = ((f32[16,3,4]{2,1,0:T(4,128)}), f32[16,3,4]{2,1,0:T(4,128)S(1)}, u32[]{:S(2)}, u32[]{:S(2)}) async-start(f32[16,3,4]{2,1,0:T(4,128)} %stack.20), calls=%async_computation | async-start | bytes 65536 | tf_op jit(solution)/shard_map/all_to_all | solution.py:99
  24.4 5.1 %copy-start.15 = (f32[64]{0:T(128)}, f32[64]{0:T(128)S(1)}, u32[]{:S(2)}) copy-start(f32[64]{0:T(128)S(1)} %add.29) | copy-start | bytes 772
  24.5 0.5 copy-start.17
  25.3 0.8 copy-start.9
  25.4 7.2 %copy-start.13 = (f32[64]{0:T(128)}, f32[64]{0:T(128)S(1)}, u32[]{:S(2)}) copy-start(f32[64]{0:T(128)S(1)} %slice_bitcast_fusion.3) | copy-start | bytes 772
  26.2 6.4 %copy-start.3 = (f32[128,64]{0,1:T(8,128)}, f32[128,64]{0,1:T(8,128)S(1)}, u32[]{:S(2)}) copy-start(f32[128,64]{0,1:T(8,128)S(1)} %copy.159) | copy-start | bytes 98308
  36.0 84.0 %all-to-all-start.1 = ((f32[64,129,64]{1,2,0:T(8,128)}), f32[64,129,64]{1,2,0:T(8,128)}, u32[]{:S(2)}, u32[]{:S(2)}) async-start(f32[64,129,64]{1,2,0:T(8,128)} %pad_maximum_fusion), calls=%async_computation.1 | async-start | bytes 8388608 | tf_op jit(solution)/shard_map/all_to_all | solution.py:69
  155.6 20.0 %copy-start.8 = (f32[128,64]{1,0:T(8,128)S(1)}, f32[128,64]{1,0:T(8,128)}, u32[]{:S(2)}) copy-start(f32[128,64]{1,0:T(8,128)} %get-tuple-element.68) | copy-start | bytes 98308
  155.6 20.1 %copy-start.7 = (f32[128,64]{1,0:T(8,128)S(1)}, f32[128,64]{1,0:T(8,128)}, u32[]{:S(2)}) copy-start(f32[128,64]{1,0:T(8,128)} %get-tuple-element.70) | copy-start | bytes 98308
  155.6 20.1 %copy-start.10 = (f32[64,128]{1,0:T(8,128)S(1)}, f32[64,128]{1,0:T(8,128)}, u32[]{:S(2)}) copy-start(f32[64,128]{1,0:T(8,128)} %copy-done.9) | copy-start | bytes 98308
  155.6 61.2 %all-to-all-start.2 = ((f32[64,128,64]{1,2,0:T(8,128)}), f32[64,128,64]{1,2,0:T(8,128)}, u32[]{:S(2)}, u32[]{:S(2)}) async-start(f32[64,128,64]{1,2,0:T(8,128)} %copy.168), calls=%async_computation.2 | async-start | bytes 4194304 | tf_op jit(solution)/shard_map/all_to_all | solution.py:93
  175.3 7.6 %copy-start.12 = (pred[128,128]{0,1:T(8,128)(4,1)}, pred[128,128]{0,1:T(8,128)(4,1)S(1)}, u32[]{:S(2)}) copy-start(pred[128,128]{0,1:T(8,128)(4,1)S(1)} %iota_compare_fusion) | copy-start | bytes 49156
  175.7 49.6 %copy-start.5 = (f32[128,64]{0,1:T(8,128)}, f32[128,64]{0,1:T(8,128)S(1)}, u32[]{:S(2)}) copy-start(f32[128,64]{0,1:T(8,128)S(1)} %copy.173) | copy-start | bytes 98308
  220.5 4.8 %copy-start = (f32[64,64,64]{1,2,0:T(8,128)}, f32[64,64,64]{1,2,0:T(8,128)S(1)}, u32[]{:S(2)}) copy-start(f32[64,64,64]{1,2,0:T(8,128)S(1)} %get-tuple-element.64) | copy-start | bytes 3145732
  220.5 1.8 copy-start.4
  225.3 3.3 %copy-start.14 = (f32[64]{0:T(128)S(1)}, f32[64]{0:T(128)}, u32[]{:S(2)}) copy-start(f32[64]{0:T(128)} %copy-done.13) | copy-start | bytes 772
  230.9 8.0 %copy-start.6 = (f32[128,64]{0,1:T(8,128)S(1)}, f32[128,64]{0,1:T(8,128)}, u32[]{:S(2)}) copy-start(f32[128,64]{0,1:T(8,128)} %copy-done.5) | copy-start | bytes 98308
  239.0 2.8 copy-start.16
  239.0 2.8 copy-start.18
  239.0 3.8 %copy-start.19 = (f32[1,64]{1,0:T(1,128)S(1)}, f32[1,64]{1,0:T(1,128)}, u32[]{:S(2)}) copy-start(f32[1,64]{1,0:T(1,128)} %exp.68) | copy-start | bytes 772
  241.5 85.3 %copy-start.1 = (f32[8,128,128]{1,2,0:T(8,128)S(1)}, f32[8,128,128]{1,2,0:T(8,128)}, u32[]{:S(2)}) copy-start(f32[8,128,128]{1,2,0:T(8,128)} %get-tuple-element.51) | copy-start | bytes 1572868
